TPU v7x, 256 devices: a whole 4x4x8 slice. The times are simulated.
256 devices in a mesh: row: 8 (over z), col: 32 (over y, x, core).
Axes of the slice: x: 4, y: 4, z: 8, core: 2. Of those that a mesh axis runs over, the one named last changes fastest.
Arguments:
- tokens: bfloat16 [512, 8192], P('col', 'row'), may hold values from -6 to 6
- cotangent: bfloat16 [512, 8192], P('col', 'row'), may hold values from -6 to 6
- w_gate: bfloat16 [8192, 16384], P('row', 'col'), may hold values from -0.09375 to 0.09375
- w_up: bfloat16 [8192, 16384], P('row', 'col'), may hold values from -0.09375 to 0.09375
- w_down: bfloat16 [16384, 8192], P('col', 'row'), may hold values from -0.0625 to 0.0625
- order_gate: int32 [2048], replicated, may hold values from 0 to 2047, each once
- order_up: int32 [2048], replicated, may hold values from 0 to 2047, each once
- order_down: int32 [2048], replicated, may hold values from 0 to 2047, each once
Outputs:
- output: bfloat16 [512, 8192], P('col', 'row')
- input_grad: bfloat16 [512, 8192], P('col', 'row')
- gate_weight_grad: float32 [8192, 16384], P('row', 'col')
- up_weight_grad: float32 [8192, 16384], P('row', 'col')
- down_weight_grad: float32 [16384, 8192], P('col', 'row')
Inputs may be any that keep to these rules, and one draw needn't show every extreme that they name: `order_gate`: each of the 2048 block numbers appears exactly once. `order_up`: each of the 2048 block numbers appears exactly once. `order_down`: each of the 2048 block numbers appears exactly once.
All inputs are finite; a program needn't handle non-finite values.
Results may differ from a plain program's by a relative error of at most 0.0049.
Values may be sent and summed in bfloat16 or wider, within the bound.
No kernel may reach another device: no remote copies, remote signals or barrier semaphores. Data moves between devices by JAX's collectives and lax.ppermute only.
A program may use at most 64 MiB of HBM per device.

v0:
```python
import jax
import jax.numpy as jnp
from jax import lax
from jax.sharding import PartitionSpec as P

BLOCK = 256


def kept_table(order, row_first, col_first, row_count, col_count, stride):
    kept_count = order.shape[0] // 2
    row_ids = row_first + jnp.arange(row_count, dtype=jnp.int32)
    col_ids = col_first + jnp.arange(col_count, dtype=jnp.int32)
    block_ids = row_ids[:, None] * stride + col_ids[None, :]
    return jnp.any(block_ids[:, :, None] == order[:kept_count][None, None, :], axis=2)


def expand_mask(kept_mask):
    row_count, col_count = kept_mask.shape
    spread = jnp.broadcast_to(kept_mask[:, None, :, None], (row_count, BLOCK, col_count, BLOCK))
    return spread.reshape(row_count * BLOCK, col_count * BLOCK)


def dense_apply(left_operand, right_operand, kept_mask, product_kind):
    full_mask = expand_mask(kept_mask)
    if product_kind == "forward":
        masked = right_operand * full_mask.astype(right_operand.dtype)
        return jnp.dot(left_operand, masked, preferred_element_type=jnp.float32)
    if product_kind == "transposed":
        masked = right_operand * full_mask.astype(right_operand.dtype)
        return lax.dot_general(
            left_operand, masked, (((1,), (1,)), ((), ())), preferred_element_type=jnp.float32
        )
    product = lax.dot_general(
        left_operand, right_operand, (((0,), (0,)), ((), ())), preferred_element_type=jnp.float32
    )
    return product * full_mask.astype(jnp.float32)


def apply_blocks(left_operand, right_operand, kept_mask, product_kind):
    return dense_apply(left_operand, right_operand, kept_mask, product_kind)


def on_device(tokens, cotangent, w_gate, w_up, w_down, order_gate, order_up, order_down):
    rows_here = w_gate.shape[0] // BLOCK
    cols_here = w_gate.shape[1] // BLOCK
    row_start = lax.axis_index("row") * rows_here
    col_start = lax.axis_index("col") * cols_here
    width_blocks = rows_here * lax.axis_size("row")
    hidden_blocks = cols_here * lax.axis_size("col")
    keep_gate = kept_table(order_gate, row_start, col_start, rows_here, cols_here, hidden_blocks)
    keep_up = kept_table(order_up, row_start, col_start, rows_here, cols_here, hidden_blocks)
    keep_down = kept_table(order_down, col_start, row_start, cols_here, rows_here, width_blocks)
    tokens_all = lax.all_gather(tokens, "col", axis=0, tiled=True)
    gate_term = apply_blocks(tokens_all, w_gate, keep_gate, "forward")
    up_term = apply_blocks(tokens_all, w_up, keep_up, "forward")
    gate, up = (
        lax.psum_scatter(gate_term, "row", scatter_dimension=0, tiled=True),
        lax.psum_scatter(up_term, "row", scatter_dimension=0, tiled=True),
    )
    sigmoid_gate = jax.nn.sigmoid(gate)
    activation = gate * sigmoid_gate
    hidden = (activation * up).astype(jnp.bfloat16)
    hidden_all = lax.all_gather(hidden, "row", axis=0, tiled=True)
    output_term = apply_blocks(hidden_all, w_down, keep_down, "forward")
    output = lax.psum_scatter(output_term, "col", scatter_dimension=0, tiled=True).astype(
        jnp.bfloat16
    )
    cotangent_all = lax.all_gather(cotangent, "col", axis=0, tiled=True)
    hidden_term = apply_blocks(cotangent_all, w_down, keep_down, "transposed")
    hidden_grad = lax.psum_scatter(hidden_term, "row", scatter_dimension=0, tiled=True)
    gate_grad = (hidden_grad * up * sigmoid_gate * (1.0 + gate * (1.0 - sigmoid_gate))).astype(
        jnp.bfloat16
    )
    up_grad = (hidden_grad * activation).astype(jnp.bfloat16)
    gate_grad_all, up_grad_all = (
        lax.all_gather(gate_grad, "row", axis=0, tiled=True),
        lax.all_gather(up_grad, "row", axis=0, tiled=True),
    )
    down_weight_grad = apply_blocks(hidden_all, cotangent_all, keep_down, "weights")
    gate_weight_grad = apply_blocks(tokens_all, gate_grad_all, keep_gate, "weights")
    up_weight_grad = apply_blocks(tokens_all, up_grad_all, keep_up, "weights")
    through_gate = apply_blocks(gate_grad_all, w_gate, keep_gate, "transposed")
    through_up = apply_blocks(up_grad_all, w_up, keep_up, "transposed")
    gate_share = lax.psum_scatter(through_gate, "col", scatter_dimension=0, tiled=True)
    up_share = lax.psum_scatter(through_up, "col", scatter_dimension=0, tiled=True)
    input_grad = gate_share + up_share
    return (
        output,
        input_grad.astype(jnp.bfloat16),
        gate_weight_grad,
        up_weight_grad,
        down_weight_grad,
    )


def solution(mesh):
    placed = (
        P("col", "row"),
        P("col", "row"),
        P("row", "col"),
        P("row", "col"),
        P("col", "row"),
        P(),
        P(),
        P(),
    )
    return jax.shard_map(
        on_device,
        mesh=mesh,
        in_specs=placed,
        out_specs=(
            P("col", "row"),
            P("col", "row"),
            P("row", "col"),
            P("row", "col"),
            P("col", "row"),
        ),
        check_vma=False,
    )
```

profile of v0, /device:TPU:2, one launch (start us, length us, event | category | flops | bytes accessed | tf_op | source)
XLA Modules:
  0.0 445.8 jit_solution(2200922386354329133)
XLA Ops:
  10.3 50.4 %all-gather.5.cloned.1.call-done = bf16[512,1024]{1,0:T(8,128)(2,1)} async-done(((bf16[16,1024]{1,0:T(8,128)(2,1)}), bf16[512,1024]{1,0:T(8,128)(2,1)}) %all-gather.5.cloned.1.call-update) | async-done | bytes 1048592 | tf_op jit(solution)/shard_map/all_gather | solution.py:68
  60.8 2.3 convolution_bitcast_fusion
  65.9 44.4 %all-gather.3.cloned.1.call-done = bf16[512,1024]{1,0:T(8,128)(2,1)} async-done(((bf16[16,1024]{1,0:T(8,128)(2,1)}), bf16[512,1024]{1,0:T(8,128)(2,1)}) %all-gather.3.cloned.1.call-update) | async-done | bytes 1048592 | tf_op jit(solution)/shard_map/all_gather | solution.py:53
  110.3 2.0 convolution_bitcast_fusion.2
  114.3 1.7 copy.34
  116.0 2.9 convolution_bitcast_fusion.1
  118.9 2.5 copy.44
  121.6 30.7 %reduce-scatter.20.cloned.1.call-done = f32[64,512]{1,0:T(8,128)} async-done(((f32[512,512]{1,0:T(8,128)}), f32[64,512]{1,0:T(8,128)}) %reduce-scatter.20.cloned.1.call-update) | async-done | bytes 131088 | tf_op jit(solution)/shard_map/reduce_scatter | solution.py:70
  152.3 40.6 %reduce-scatter.16.cloned.1.call-done = f32[64,512]{1,0:T(8,128)} async-done(((f32[512,512]{1,0:T(8,128)}), f32[64,512]{1,0:T(8,128)}) %reduce-scatter.16.cloned.1.call-update) | async-done | bytes 131088 | tf_op jit(solution)/shard_map/reduce_scatter | solution.py:57
  192.9 40.0 %reduce-scatter.18.cloned.1.call-done = f32[64,512]{1,0:T(8,128)} async-done(((f32[512,512]{1,0:T(8,128)}), f32[64,512]{1,0:T(8,128)}) %reduce-scatter.18.cloned.1.call-update) | async-done | bytes 131088 | tf_op jit(solution)/shard_map/reduce_scatter | solution.py:58
  234.1 25.5 %all_gather.16 = bf16[512,512]{1,0:T(8,128)(2,1)S(1)} all-gather(bf16[64,512]{1,0:T(8,128)(2,1)S(1)} %get-tuple-element.29), channel_id=1, replica_groups=mesh['row'=8,'col'=32] {'row'}, dimensions={0}, use_global_device_ids=true | all-gather | bytes 589824 | tf_op jit(solution)/shard_map/all_gather | solution.py:63
  259.6 3.3 fusion.1
  262.9 25.5 %all_gather.18 = bf16[512,512]{1,0:T(8,128)(2,1)S(1)} all-gather(bf16[64,512]{1,0:T(8,128)(2,1)S(1)} %get-tuple-element.28), channel_id=1, replica_groups=mesh['row'=8,'col'=32] {'row'}, dimensions={0}, use_global_device_ids=true | all-gather | bytes 589824 | tf_op jit(solution)/shard_map/all_gather | solution.py:76
  288.4 25.2 %all_gather.19 = bf16[512,512]{1,0:T(8,128)(2,1)S(1)} all-gather(bf16[64,512]{1,0:T(8,128)(2,1)S(1)} %get-tuple-element.27), channel_id=1, replica_groups=mesh['row'=8,'col'=32] {'row'}, dimensions={0}, use_global_device_ids=true | all-gather | bytes 589824 | tf_op jit(solution)/shard_map/all_gather | solution.py:77
  313.7 2.0 fusion.9
  315.7 2.1 convolution_add_fusion
  319.1 2.0 bitcast_select_fusion.1
  321.2 3.0 copy.40
  324.2 2.1 bitcast_select_fusion
  326.2 3.0 copy.41
  329.2 2.0 convolution_select_fusion
  331.3 16.4 %reduce-scatter.12.cloned.1.call-done = f32[16,1024]{1,0:T(8,128)} async-done(((f32[512,1024]{1,0:T(8,128)}), f32[16,1024]{1,0:T(8,128)}) %reduce-scatter.12.cloned.1.call-update) | async-done | bytes 65552 | tf_op jit(solution)/shard_map/reduce_scatter | solution.py:65
  349.1 88.4 %reduce-scatter.14.cloned.1.call-done = f32[16,1024]{1,0:T(8,128)} async-done(((f32[512,1024]{1,0:T(8,128)}), f32[16,1024]{1,0:T(8,128)}) %reduce-scatter.14.cloned.1.call-update) | async-done | bytes 65552 | tf_op jit(solution)/shard_map/reduce_scatter | solution.py:84
  437.5 1.5 convert_element_type.28
  (60 shorter events, 12.0 us)
Async XLA Ops:
  7.2 53.6 %all-gather.5.cloned.1.call-start = ((), (), s32[]{:S(2)}) async-start(), calls=%async_computation.7 | async-start | bytes 1081344 | tf_op jit(solution)/shard_map/all_gather | solution.py:68
  7.9 102.4 %all-gather.3.cloned.1.call-start = ((), (), s32[]{:S(2)}) async-start(), calls=%async_computation.5 | async-start | bytes 1081344 | tf_op jit(solution)/shard_map/all_gather | solution.py:53
  8.6 143.6 %reduce-scatter.20.cloned.1.call-start = ((), (), s32[]{:S(2)}) async-start(), calls=%async_computation.11 | async-start | bytes 1179648 | tf_op jit(solution)/shard_map/reduce_scatter | solution.py:70
  10.3 249.3 %copy-start.5 = (pred[64,8,4,256]{3,1,2,0:T(8,128)(4,1)}, pred[64,8,4,256]{3,1,2,0:T(8,128)(4,1)S(1)}, u32[]{:S(2)}) copy-start(pred[64,8,4,256]{3,1,2,0:T(8,128)(4,1)S(1)} %copy.50) | copy-start | bytes 1572868
  63.0 1.5 slice-start
  63.1 1.5 slice-start.1
  63.1 2.3 copy-start.9
  64.4 128.5 %reduce-scatter.16.cloned.1.call-start = ((), (), s32[]{:S(2)}) async-start(), calls=%async_computation.9 | async-start | bytes 1179648 | tf_op jit(solution)/shard_map/reduce_scatter | solution.py:57
  65.4 46.9 %copy-start.7 = (pred[64,8,4,256]{3,1,2,0:T(8,128)(4,1)}, pred[64,8,4,256]{3,1,2,0:T(8,128)(4,1)S(1)}, u32[]{:S(2)}) copy-start(pred[64,8,4,256]{3,1,2,0:T(8,128)(4,1)S(1)} %copy.48) | copy-start | bytes 1572868
  113.6 119.3 %reduce-scatter.18.cloned.1.call-start = ((), (), s32[]{:S(2)}) async-start(), calls=%async_computation.10 | async-start | bytes 1179648 | tf_op jit(solution)/shard_map/reduce_scatter | solution.py:58
  114.3 4.6 %copy-start = (pred[64,8,4,256]{3,1,2,0:T(8,128)(4,1)}, pred[64,8,4,256]{3,1,2,0:T(8,128)(4,1)S(1)}, u32[]{:S(2)}) copy-start(pred[64,8,4,256]{3,1,2,0:T(8,128)(4,1)S(1)} %copy.49) | copy-start | bytes 1572868
  121.5 226.2 %reduce-scatter.12.cloned.1.call-start = ((), (), s32[]{:S(2)}) async-start(), calls=%async_computation.6 | async-start | bytes 2162688 | tf_op jit(solution)/shard_map/reduce_scatter | solution.py:65
  262.9 174.6 %reduce-scatter.14.cloned.1.call-start = ((), (), s32[]{:S(2)}) async-start(), calls=%async_computation.8 | async-start | bytes 2162688 | tf_op jit(solution)/shard_map/reduce_scatter | solution.py:84
  313.7 2.0 copy-start.3
  313.7 2.0 copy-start.1
  317.7 1.0 copy-start.8
  317.7 1.4 copy-start.11
  321.2 3.0 copy-start.2
  321.2 3.0 copy-start.4
  326.2 3.0 copy-start.6
  326.2 3.0 copy-start.10
Sparse Core Ops, SparseCore 0:
  10.5 50.1 all-gather.4
  63.3 46.9 all-gather.2
  113.4 38.7 reduce-scatter.19
  155.2 37.6 reduce-scatter.15
  195.3 37.6 reduce-scatter.17
  263.0 84.6 reduce-scatter.11
  351.5 85.9 reduce-scatter.13
where the time goes:
time: 446 us
  waiting for transfers between devices  312 us (70%)
  blocking collectives  76.2 us (17%)
  matrix products  20.7 us (5%)
  local copies, waits for them, and re-layouts  17.3 us (4%)
  between operations  14.3 us (3%)
  other arithmetic  4.62 us (1%)
    reduce_scatter x1, waiting for transfers between devices, on_device(): lax.psum_scatter(through_gate, 'col', scatter_dimension=0, tiled=True)  88.4 us
    all_gather x1, waiting for transfers between devices, on_device(): cotangent_all = lax.all_gather(cotangent, 'col', axis=0, tiled=True)  50.4 us
    all_gather x1, waiting for transfers between devices, on_device(): tokens_all = lax.all_gather(tokens, 'col', axis=0, tiled=True)  44.4 us
    reduce_scatter x1, waiting for transfers between devices, on_device(): lax.psum_scatter(gate_term, 'row', scatter_dimension=0, tiled=True)  40.6 us
    reduce_scatter x1, waiting for transfers between devices, on_device(): lax.psum_scatter(up_term, 'row', scatter_dimension=0, tiled=True)  40 us
    reduce_scatter x1, waiting for transfers between devices, on_device(): lax.psum_scatter(hidden_term, 'row', scatter_dimension=0, tiled=True)  30.7 us
    all_gather x1, blocking collectives, on_device(): hidden_all = lax.all_gather(hidden, 'row', axis=0, tiled=True)  25.5 us
    all_gather x1, blocking collectives, on_device(): lax.all_gather(gate_grad, 'row', axis=0, tiled=True)  25.5 us
  transfers between devices with their start and end apart: 7, of which 7 were waited for; matrix products, arithmetic and copies ran while one was open for 8% of the time, Pallas kernels for 0%

commit v1 on v0

--- a/solution.py
+++ b/solution.py
@@ -60,7 +60,16 @@
     sigmoid_gate = jax.nn.sigmoid(gate)
     activation = gate * sigmoid_gate
     hidden = (activation * up).astype(jnp.bfloat16)
-    hidden_all = lax.all_gather(hidden, "row", axis=0, tiled=True)
+    ways = lax.axis_size("row")
+    up_2 = [(d, (d + 1) % ways) for d in range(ways)]
+    down = [(d, (d - 1) % ways) for d in range(ways)]
+    earlier, later = ([hidden], [hidden])
+    for _ in range(ways // 2):
+        earlier.append(lax.ppermute(earlier[-1], "row", up_2))
+    for _ in range((ways - 1) // 2):
+        later.append(lax.ppermute(later[-1], "row", down))
+    line = jnp.concatenate([*earlier[::-1], *later[1:]], axis=0)
+    hidden_all = jnp.roll(line, (lax.axis_index("row") - ways // 2) * hidden.shape[0], axis=0)
     output_term = apply_blocks(hidden_all, w_down, keep_down, "forward")
     output = lax.psum_scatter(output_term, "col", scatter_dimension=0, tiled=True).astype(
         jnp.bfloat16

time: 446 us -> 473 us (1.061)
  waiting for transfers between devices: 312 us -> 354 us
  blocking collectives: 76.2 us -> 51.1 us
  starting transfers between devices: 0.28 us -> 10.3 us
    reduce_scatter x1, waiting for transfers between devices: 16.4 us -> 88.4 us  [on_device(): lax.psum_scatter(output_term, 'col', scatter_dimension=0, tiled=True)]
    reduce_scatter x1, waiting for transfers between devices: 88.4 us -> 46.1 us  [on_device(): lax.psum_scatter(through_gate, 'col', scatter_dimension=0, tiled=True)]
    all_gather x1 -> x0, blocking collectives: 25.5 us -> none  [on_device(): hidden_all = lax.all_gather(hidden, 'row', axis=0, tiled=True)]
    ppermute x0 -> x7, waiting for transfers between devices: none -> 12 us  [the longest x4 12 us: on_device(): earlier.append(lax.ppermute(earlier[-1], 'row', up_2))]
    ppermute x0 -> x7, starting transfers between devices: none -> 10 us  [the longest x3 9.7 us: on_device(): later.append(lax.ppermute(later[-1], 'row', down))]
    unnamed x34 -> x43, local copies, waits for them, and re-layouts: 15.5 us -> 15.2 us
  transfers between devices with their start and end apart: 7 -> 14, of which waited for: 7 -> 11; matrix products, arithmetic and copies ran while one was open for 8% -> 7% of each run, Pallas kernels for 0% -> 0%
where the time goes in v1:
time: 473 us; the launch traced here: 472 us
  waiting for transfers between devices  354 us (75%)
  blocking collectives  51.1 us (11%)
  matrix products  20.5 us (4%)
  local copies, waits for them, and re-layouts  16.9 us (4%)
  between operations  14.4 us (3%)
  starting transfers between devices  10.3 us (2%)
    reduce_scatter x1, waiting for transfers between devices, on_device(): lax.psum_scatter(output_term, 'col', scatter_dimension=0, tiled=True)  88.4 us
    all_gather x1, waiting for transfers between devices, on_device(): cotangent_all = lax.all_gather(cotangent, 'col', axis=0, tiled=True)  50.4 us
    reduce_scatter x1, waiting for transfers between devices, on_device(): lax.psum_scatter(through_gate, 'col', scatter_dimension=0, tiled=True)  46.1 us
    all_gather x1, waiting for transfers between devices, on_device(): tokens_all = lax.all_gather(tokens, 'col', axis=0, tiled=True)  44.4 us
    reduce_scatter x1, waiting for transfers between devices, on_device(): lax.psum_scatter(gate_term, 'row', scatter_dimension=0, tiled=True)  40.6 us
    reduce_scatter x1, waiting for transfers between devices, on_device(): lax.psum_scatter(up_term, 'row', scatter_dimension=0, tiled=True)  40 us
    reduce_scatter x1, waiting for transfers between devices, on_device(): lax.psum_scatter(hidden_term, 'row', scatter_dimension=0, tiled=True)  30.9 us
    all_gather x1, blocking collectives, on_device(): lax.all_gather(up_grad, 'row', axis=0, tiled=True)  25.6 us
  transfers between devices with their start and end apart: 14, of which 11 were waited for; matrix products, arithmetic and copies ran while one was open for 7% of the time, Pallas kernels for 0%

profile of v1, /device:TPU:2, one launch (start us, length us, event | category | flops | bytes accessed | tf_op | source)
XLA Modules:
  0.0 472.2 jit_solution(70404814825232081)
XLA Ops:
  10.3 50.4 %all-gather.5.cloned.1.call-done = bf16[512,1024]{1,0:T(8,128)(2,1)} async-done(((bf16[16,1024]{1,0:T(8,128)(2,1)}), bf16[512,1024]{1,0:T(8,128)(2,1)}) %all-gather.5.cloned.1.call-update) | async-done | bytes 1048592 | tf_op jit(solution)/shard_map/all_gather | solution.py:77
  60.8 2.3 convolution_bitcast_fusion
  66.0 44.4 %all-gather.3.cloned.1.call-done = bf16[512,1024]{1,0:T(8,128)(2,1)} async-done(((bf16[16,1024]{1,0:T(8,128)(2,1)}), bf16[512,1024]{1,0:T(8,128)(2,1)}) %all-gather.3.cloned.1.call-update) | async-done | bytes 1048592 | tf_op jit(solution)/shard_map/all_gather | solution.py:53
  115.8 2.9 convolution_bitcast_fusion.1
  118.7 2.5 copy.42
  121.4 30.9 %reduce-scatter.20.cloned.1.call-done = f32[64,512]{1,0:T(8,128)} async-done(((f32[512,512]{1,0:T(8,128)}), f32[64,512]{1,0:T(8,128)}) %reduce-scatter.20.cloned.1.call-update) | async-done | bytes 131088 | tf_op jit(solution)/shard_map/reduce_scatter | solution.py:79
  152.3 40.6 %reduce-scatter.16.cloned.1.call-done = f32[64,512]{1,0:T(8,128)} async-done(((f32[512,512]{1,0:T(8,128)}), f32[64,512]{1,0:T(8,128)}) %reduce-scatter.16.cloned.1.call-update) | async-done | bytes 131088 | tf_op jit(solution)/shard_map/reduce_scatter | solution.py:57
  192.9 40.0 %reduce-scatter.18.cloned.1.call-done = f32[64,512]{1,0:T(8,128)} async-done(((f32[512,512]{1,0:T(8,128)}), f32[64,512]{1,0:T(8,128)}) %reduce-scatter.18.cloned.1.call-update) | async-done | bytes 131088 | tf_op jit(solution)/shard_map/reduce_scatter | solution.py:58
  234.1 25.6 %all_gather.14 = bf16[512,512]{1,0:T(8,128)(2,1)S(1)} all-gather(bf16[64,512]{1,0:T(8,128)(2,1)S(1)} %get-tuple-element.28), channel_id=1, replica_groups=mesh['row'=8,'col'=32] {'row'}, dimensions={0}, use_global_device_ids=true | all-gather | bytes 589824 | tf_op jit(solution)/shard_map/all_gather | solution.py:85
  261.4 25.6 %all_gather.15 = bf16[512,512]{1,0:T(8,128)(2,1)S(1)} all-gather(bf16[64,512]{1,0:T(8,128)(2,1)S(1)} %get-tuple-element.27), channel_id=1, replica_groups=mesh['row'=8,'col'=32] {'row'}, dimensions={0}, use_global_device_ids=true | all-gather | bytes 589824 | tf_op jit(solution)/shard_map/all_gather | solution.py:86
  286.9 2.1 convolution_add_fusion
  289.4 5.3 %collective-permute-done = bf16[64,512]{1,0:T(8,128)(2,1)S(1)} collective-permute-done((bf16[64,512]{1,0:T(8,128)(2,1)S(1)}, bf16[64,512]{1,0:T(8,128)(2,1)S(1)}, u32[]{:S(2)}, u32[]{:S(2)}) %collective-permute-start) | collective-permute-done | bytes 65568 | tf_op jit(solution)/shard_map/ppermute | solution.py:68
  294.7 3.2 collective-permute-start.4
  297.9 2.2 collective-permute-done.1
  300.1 3.2 collective-permute-start.5
  303.4 2.2 collective-permute-done.2
  305.6 3.2 collective-permute-start.6
  308.9 2.2 collective-permute-done.3
  312.3 2.0 fusion.1
  315.7 2.0 bitcast_select_fusion.1
  317.8 2.9 copy.38
  324.5 3.4 convolution_select_fusion
  327.9 46.1 %reduce-scatter.14.cloned.1.call-done = f32[16,1024]{1,0:T(8,128)} async-done(((f32[512,1024]{1,0:T(8,128)}), f32[16,1024]{1,0:T(8,128)}) %reduce-scatter.14.cloned.1.call-update) | async-done | bytes 65552 | tf_op jit(solution)/shard_map/reduce_scatter | solution.py:93
  375.5 88.4 %reduce-scatter.12.cloned.1.call-done = f32[16,1024]{1,0:T(8,128)} async-done(((f32[512,1024]{1,0:T(8,128)}), f32[16,1024]{1,0:T(8,128)}) %reduce-scatter.12.cloned.1.call-update) | async-done | bytes 65552 | tf_op jit(solution)/shard_map/reduce_scatter | solution.py:74
  (83 shorter events, 23.8 us)
Async XLA Ops:
  7.2 53.6 %all-gather.5.cloned.1.call-start = ((), (), s32[]{:S(2)}) async-start(), calls=%async_computation.7 | async-start | bytes 1081344 | tf_op jit(solution)/shard_map/all_gather | solution.py:77
  7.9 102.4 %all-gather.3.cloned.1.call-start = ((), (), s32[]{:S(2)}) async-start(), calls=%async_computation.5 | async-start | bytes 1081344 | tf_op jit(solution)/shard_map/all_gather | solution.py:53
  8.6 143.6 %reduce-scatter.20.cloned.1.call-start = ((), (), s32[]{:S(2)}) async-start(), calls=%async_computation.11 | async-start | bytes 1179648 | tf_op jit(solution)/shard_map/reduce_scatter | solution.py:79
  10.3 52.7 %copy-start.3 = (pred[64,8,4,256]{3,1,2,0:T(8,128)(4,1)}, pred[64,8,4,256]{3,1,2,0:T(8,128)(4,1)S(1)}, u32[]{:S(2)}) copy-start(pred[64,8,4,256]{3,1,2,0:T(8,128)(4,1)S(1)} %copy.48) | copy-start | bytes 1572868
  63.1 1.5 slice-start
  63.1 1.5 slice-start.1
  63.1 2.3 copy-start.2
  64.4 128.5 %reduce-scatter.16.cloned.1.call-start = ((), (), s32[]{:S(2)}) async-start(), calls=%async_computation.9 | async-start | bytes 1179648 | tf_op jit(solution)/shard_map/reduce_scatter | solution.py:57
  65.4 48.3 %copy-start = (pred[64,8,4,256]{3,1,2,0:T(8,128)(4,1)}, pred[64,8,4,256]{3,1,2,0:T(8,128)(4,1)S(1)}, u32[]{:S(2)}) copy-start(pred[64,8,4,256]{3,1,2,0:T(8,128)(4,1)S(1)} %copy.46) | copy-start | bytes 1572868
  113.6 119.3 %reduce-scatter.18.cloned.1.call-start = ((), (), s32[]{:S(2)}) async-start(), calls=%async_computation.10 | async-start | bytes 1179648 | tf_op jit(solution)/shard_map/reduce_scatter | solution.py:58
  121.3 252.7 %reduce-scatter.14.cloned.1.call-start = ((), (), s32[]{:S(2)}) async-start(), calls=%async_computation.8 | async-start | bytes 2162688 | tf_op jit(solution)/shard_map/reduce_scatter | solution.py:93
  289.0 23.3 %copy-start.4 = (pred[64,8,4,256]{3,1,2,0:T(8,128)(4,1)S(1)}, pred[64,8,4,256]{3,1,2,0:T(8,128)(4,1)}, u32[]{:S(2)}) copy-start(pred[64,8,4,256]{3,1,2,0:T(8,128)(4,1)} %copy-done.3) | copy-start | bytes 1572868
  289.1 174.8 %reduce-scatter.12.cloned.1.call-start = ((), (), s32[]{:S(2)}) async-start(), calls=%async_computation.6 | async-start | bytes 2162688 | tf_op jit(solution)/shard_map/reduce_scatter | solution.py:74
  289.1 5.6 %collective-permute-start = (bf16[64,512]{1,0:T(8,128)(2,1)S(1)}, bf16[64,512]{1,0:T(8,128)(2,1)S(1)}, u32[]{:S(2)}, u32[]{:S(2)}) collective-permute-start(bf16[64,512]{1,0:T(8,128)(2,1)S(1)} %get-tuple-element.29), channel_id=1, source_target_pairs={{0,32},{32,64},{64,96},{96,128},{128,160},{160,192},{192,224},{224... | collective-permute-start | bytes 196616 | tf_op jit(solution)/shard_map/ppermute | solution.py:68
  294.7 5.5 %collective-permute-start.1 = (bf16[64,512]{1,0:T(8,128)(2,1)S(1)}, bf16[64,512]{1,0:T(8,128)(2,1)S(1)}, u32[]{:S(2)}, u32[]{:S(2)}) collective-permute-start(bf16[64,512]{1,0:T(8,128)(2,1)S(1)} %collective-permute-done), channel_id=1, source_target_pairs={{0,32},{32,64},{64,96},{96,128},{128,160},{160,192},{192,224},{224... | collective-permute-start | bytes 196616 | tf_op jit(solution)/shard_map/ppermute | solution.py:68
  294.7 5.5 %collective-permute-start.4 = (bf16[64,512]{1,0:T(8,128)(2,1)S(1)}, bf16[64,512]{1,0:T(8,128)(2,1)S(1)}, u32[]{:S(2)}, u32[]{:S(2)}) collective-permute-start(bf16[64,512]{1,0:T(8,128)(2,1)S(1)} %get-tuple-element.29), channel_id=1, source_target_pairs={{0,224},{32,0},{64,32},{96,64},{128,96},{160,128},{192,160},{224,1... | collective-permute-start | bytes 196616 | tf_op jit(solution)/shard_map/ppermute | solution.py:70
  300.1 5.5 %collective-permute-start.2 = (bf16[64,512]{1,0:T(8,128)(2,1)S(1)}, bf16[64,512]{1,0:T(8,128)(2,1)S(1)}, u32[]{:S(2)}, u32[]{:S(2)}) collective-permute-start(bf16[64,512]{1,0:T(8,128)(2,1)S(1)} %collective-permute-done.1), channel_id=1, source_target_pairs={{0,32},{32,64},{64,96},{96,128},{128,160},{160,192},{192,224},{224... | collective-permute-start | bytes 196616 | tf_op jit(solution)/shard_map/ppermute | solution.py:68
  300.1 5.5 %collective-permute-start.5 = (bf16[64,512]{1,0:T(8,128)(2,1)S(1)}, bf16[64,512]{1,0:T(8,128)(2,1)S(1)}, u32[]{:S(2)}, u32[]{:S(2)}) collective-permute-start(bf16[64,512]{1,0:T(8,128)(2,1)S(1)} %collective-permute-done.4), channel_id=1, source_target_pairs={{0,224},{32,0},{64,32},{96,64},{128,96},{160,128},{192,160},{224,1... | collective-permute-start | bytes 196616 | tf_op jit(solution)/shard_map/ppermute | solution.py:70
  305.6 5.5 %collective-permute-start.3 = (bf16[64,512]{1,0:T(8,128)(2,1)S(1)}, bf16[64,512]{1,0:T(8,128)(2,1)S(1)}, u32[]{:S(2)}, u32[]{:S(2)}) collective-permute-start(bf16[64,512]{1,0:T(8,128)(2,1)S(1)} %collective-permute-done.2), channel_id=1, source_target_pairs={{0,32},{32,64},{64,96},{96,128},{128,160},{160,192},{192,224},{224... | collective-permute-start | bytes 196616 | tf_op jit(solution)/shard_map/ppermute | solution.py:68
  305.6 6.7 %copy-start.7 = (bf16[512,1024]{1,0:T(8,128)(2,1)S(1)}, bf16[512,1024]{1,0:T(8,128)(2,1)}, u32[]{:S(2)}) copy-start(bf16[512,1024]{1,0:T(8,128)(2,1)} %param.12) | copy-start | bytes 3145732
  305.6 5.6 %collective-permute-start.6 = (bf16[64,512]{1,0:T(8,128)(2,1)S(1)}, bf16[64,512]{1,0:T(8,128)(2,1)S(1)}, u32[]{:S(2)}, u32[]{:S(2)}) collective-permute-start(bf16[64,512]{1,0:T(8,128)(2,1)S(1)} %collective-permute-done.5), channel_id=1, source_target_pairs={{0,224},{32,0},{64,32},{96,64},{128,96},{160,128},{192,160},{224,1... | collective-permute-start | bytes 196616 | tf_op jit(solution)/shard_map/ppermute | solution.py:70
  314.3 1.1 copy-start.1
  314.3 1.4 copy-start.8
  322.6 1.8 copy-start.5
  (1 other events, 1.0 us)
Sparse Core Ops, SparseCore 0:
  10.5 50.1 all-gather.4
  63.3 46.9 all-gather.2
  113.4 38.7 reduce-scatter.19
  155.2 37.6 reduce-scatter.15
  195.3 37.6 reduce-scatter.17
  289.2 84.7 reduce-scatter.13
  377.8 85.9 reduce-scatter.11
